TPU v7x, 128 devices: a whole 4x4x4 slice. The times are simulated.
128 devices in a mesh: req: 16 (over y, x), head: 8 (over z, core).
Axes of the slice: x: 4, y: 4, z: 4, core: 2. Of those that a mesh axis runs over, the one named last changes fastest.
Arguments:
- hidden_in: bfloat16 [4864, 3072], P('req', 'head'), may hold values from -6 to 6
- dec_query: bfloat16 [768, 3072], P('req', 'head'), may hold values from -5.5 to 5.5
- dec_key: bfloat16 [768, 3072], P('req', 'head'), may hold values from -6 to 6
- dec_value: bfloat16 [768, 3072], P('req', 'head'), may hold values from -6 to 6
- pre_query: bfloat16 [4096, 3072], P('req', 'head'), may hold values from -5.5 to 5.5
- pre_key: bfloat16 [4096, 3072], P('req', 'head'), may hold values from -6 to 6
- pre_value: bfloat16 [4096, 3072], P('req', 'head'), may hold values from -6 to 6
- cache_key: bfloat16 [32, 2048, 3072], P('req', None, 'head'), may hold values from -5.5 to 5.5
- cache_value: bfloat16 [32, 2048, 3072], P('req', None, 'head'), may hold values from -6 to 6
- group_of: int32 [768, 1], replicated, may hold values from 0 to 31; in each aligned block of 768 rows (0 to 767, 768 to 1535, ...) at most 48 rows name the same one
- cache_length: int32 [32], P('req'), may hold values from 256 to 2048, as said below
- stretch_start: int32 [16], P('req'), may hold values from 256 to 2048, as said below
- row_owner: int32 [4864, 1], P('req'), may hold values from 0 to 15; in each aligned block of 304 rows (0 to 303, 304 to 607, ...) at most 40 rows name the same one
- out_weight: bfloat16 [3072, 3072], P('head'), may hold values from -0.109375 to 0.109375
- norm_gain: float32 [3072], replicated, may hold values from 0.1 to 1.9
- gate_weight: bfloat16 [3072, 4096], P(None, 'head'), may hold values from -0.109375 to 0.109375
- up_weight: bfloat16 [3072, 4096], P(None, 'head'), may hold values from -0.109375 to 0.109375
- down_weight: bfloat16 [4096, 3072], P('head'), may hold values from -0.09375 to 0.09375
Outputs:
- layer_out: bfloat16 [10240, 3072], P(('req', 'head'))
Inputs may be any that keep to these rules, and one draw needn't show every extreme that they name: `group_of`: at most 48 requests share a cache group, exactly 48 in some group; every group has a request. `cache_length`: some group has all 2048 rows valid. `stretch_start`: some stretch follows all 2048 cached rows. `row_owner`: among the 304 rows of one index of req at most 40 share an owner, exactly 40 on some index.
All inputs are finite; a program needn't handle non-finite values.
Results may differ from a plain program's by a relative error of at most 0.02.
Values may be sent and summed in bfloat16 or wider, within the bound.
No kernel may reach another device: no remote copies, remote signals or barrier semaphores. Data moves between devices by JAX's collectives and lax.ppermute only.
A program may use at most 128 MiB of HBM per device.

v0:
```python
import math
import jax
import jax.numpy as jnp
from jax import lax
from jax.sharding import PartitionSpec as P

HD = 96
CAP = 48
eps_norm = 1e-05


def head_split(matrix):
    return matrix.reshape(matrix.shape[0], matrix.shape[1] // HD, HD)


def softmax_rows(scores, allowed):
    masked = jnp.where(allowed, scores, -jnp.inf)
    highest = jnp.max(masked, axis=-1, keepdims=True)
    raised = jnp.exp(masked - highest)
    return (raised / jnp.sum(raised, axis=-1, keepdims=True)).astype(jnp.bfloat16)


def on_device(
    hidden_in,
    dec_query,
    dec_key,
    dec_value,
    pre_query,
    pre_key,
    pre_value,
    cache_key,
    cache_value,
    group_of,
    cache_length,
    stretch_start,
    row_owner,
    out_weight,
    norm_gain,
    gate_weight,
    up_weight,
    down_weight,
):
    factor = 1.0 / math.sqrt(HD)
    width_here = dec_query.shape[1]
    queries_all, keys_own, values_own = (
        lax.all_gather(dec_query, "req", axis=0, tiled=True),
        lax.all_gather(dec_key, "req", axis=0, tiled=True),
        lax.all_gather(dec_value, "req", axis=0, tiled=True),
    )
    groups_here = cache_key.shape[0]
    length_cache = cache_key.shape[1]
    first_group = lax.axis_index("req") * groups_here
    members = group_of[:, 0]
    wanted = first_group + jnp.arange(groups_here, dtype=jnp.int32)
    belongs = (members[None, :] == wanted[:, None]).astype(jnp.int32)
    ranking = jnp.cumsum(belongs, axis=1) - 1
    places = jnp.arange(CAP, dtype=jnp.int32)
    chosen = (belongs[:, None, :] == 1) & (ranking[:, None, :] == places[None, :, None])
    chooser = chosen.reshape(groups_here * CAP, members.shape[0])
    stacked_in = jnp.concatenate([queries_all, keys_own, values_own], axis=1)
    picked = jnp.dot(
        chooser.astype(jnp.bfloat16), stacked_in, preferred_element_type=jnp.float32
    ).astype(jnp.bfloat16)
    positions = jnp.arange(length_cache)
    results = []
    for group_pos in range(groups_here):
        rows_block = picked[group_pos * CAP : (group_pos + 1) * CAP]
        picked_q = head_split(rows_block[:, :width_here])
        picked_k = head_split(rows_block[:, width_here : 2 * width_here])
        picked_v = head_split(rows_block[:, 2 * width_here :])
        cache_scores = (
            jnp.einsum(
                "qhd,khd->hqk",
                picked_q,
                head_split(cache_key[group_pos]),
                preferred_element_type=jnp.float32,
            )
            * factor
        )
        own_scores = (
            jnp.sum(picked_q.astype(jnp.float32) * picked_k.astype(jnp.float32), axis=-1).T * factor
        )
        scores = jnp.concatenate([cache_scores, own_scores[:, :, None]], axis=-1)
        allowed = jnp.concatenate([positions < cache_length[group_pos], jnp.ones((1,), bool)])[
            None, None, :
        ]
        weights = softmax_rows(scores, allowed)
        blended = jnp.einsum(
            "hqk,khd->qhd",
            weights[:, :, :length_cache],
            head_split(cache_value[group_pos]),
            preferred_element_type=jnp.float32,
        )
        blended = blended + weights[:, :, length_cache].astype(jnp.float32).T[
            :, :, None
        ] * picked_v.astype(jnp.float32)
        results.append(blended.reshape(CAP, width_here))
    stacked = jnp.concatenate(results, axis=0)
    spread_back = jnp.dot(chooser.astype(jnp.float32).T, stacked, precision=lax.Precision.HIGHEST)
    dec_out = lax.psum_scatter(
        spread_back.astype(jnp.bfloat16), "req", scatter_dimension=0, tiled=True
    )
    stretch_len = pre_query.shape[0]
    key_rows = jnp.concatenate([cache_key[0], pre_key], axis=0)
    value_rows = jnp.concatenate([cache_value[0], pre_value], axis=0)
    columns = jnp.arange(length_cache + stretch_len)
    row_numbers = jnp.arange(stretch_len)
    allowed_pre = jnp.where(
        columns[None, :] < length_cache,
        columns[None, :] < stretch_start[0],
        columns[None, :] - length_cache <= row_numbers[:, None],
    )
    pre_scores = (
        jnp.einsum(
            "qhd,khd->hqk",
            head_split(pre_query),
            head_split(key_rows),
            preferred_element_type=jnp.float32,
        )
        * factor
    )
    pre_weights = softmax_rows(pre_scores, allowed_pre[None])
    pre_mixed = jnp.einsum(
        "hqk,khd->qhd", pre_weights, head_split(value_rows), preferred_element_type=jnp.float32
    )
    pre_out = pre_mixed.reshape(stretch_len, width_here).astype(jnp.bfloat16)
    attn_rows = jnp.concatenate([dec_out, pre_out], axis=0)
    projected = jnp.dot(attn_rows, out_weight, preferred_element_type=jnp.float32)
    col_start = lax.axis_index("head") * width_here
    own_cols = lax.dynamic_slice_in_dim(projected, col_start, width_here, 1) + hidden_in.astype(
        jnp.float32
    )
    contribution = lax.dynamic_update_slice_in_dim(projected, own_cols, col_start, 1)
    req_count = lax.axis_size("req")
    row_count = contribution.shape[0]
    slot_rows = 8 * ((2 * row_count + 8 * req_count - 1) // (8 * req_count))
    owners = row_owner[:, 0]
    onehot_owner = (owners[:, None] == jnp.arange(req_count, dtype=jnp.int32)[None, :]).astype(
        jnp.int32
    )
    before = jnp.sum((jnp.cumsum(onehot_owner, axis=0) - 1) * onehot_owner, axis=1)
    target = owners * slot_rows + before
    placing = (
        target[None, :] == jnp.arange(req_count * slot_rows, dtype=jnp.int32)[:, None]
    ).astype(jnp.bfloat16)
    residual = lax.psum(contribution.astype(jnp.bfloat16), "head")
    outgoing = jnp.dot(placing, residual, preferred_element_type=jnp.float32).astype(jnp.bfloat16)
    arrived = lax.all_to_all(outgoing, "req", split_axis=0, concat_axis=0, tiled=True)
    arrived_wide = arrived.astype(jnp.float32)
    squares = jnp.mean(jnp.square(arrived_wide), axis=-1, keepdims=True)
    normed = (arrived_wide * lax.rsqrt(squares + eps_norm) * norm_gain).astype(jnp.bfloat16)
    gate_act = jnp.dot(normed, gate_weight, preferred_element_type=jnp.float32)
    up_act = jnp.dot(normed, up_weight, preferred_element_type=jnp.float32)
    hidden = (jax.nn.silu(gate_act) * up_act).astype(jnp.bfloat16)
    rows_here = arrived.shape[0] // lax.axis_size("head")
    down_sum = lax.psum_scatter(
        jnp.dot(hidden, down_weight, preferred_element_type=jnp.float32).astype(jnp.bfloat16),
        "head",
        scatter_dimension=0,
        tiled=True,
    ).astype(jnp.float32)
    own_rows = lax.dynamic_slice_in_dim(
        arrived_wide, lax.axis_index("head") * rows_here, rows_here, 0
    )
    return (own_rows + down_sum).astype(jnp.bfloat16)


def solution(mesh):
    placed = (
        P("req", "head"),
        P("req", "head"),
        P("req", "head"),
        P("req", "head"),
        P("req", "head"),
        P("req", "head"),
        P("req", "head"),
        P("req", None, "head"),
        P("req", None, "head"),
        P(),
        P("req"),
        P("req"),
        P("req", None),
        P("head", None),
        P(),
        P(None, "head"),
        P(None, "head"),
        P("head", None),
    )
    return jax.shard_map(
        on_device, mesh=mesh, in_specs=placed, out_specs=P(("req", "head"), None), check_vma=False
    )
```

profile of v0, /device:TPU:0, one launch (start us, length us, event | category | flops | bytes accessed | tf_op | source)
XLA Modules:
  0.0 390.3 jit_solution(7005297331430344854)
XLA Ops:
  6.6 1.5 fusion.83
  8.1 0.7 iota_compare_fusion.8
  8.8 1.3 iota_compare_fusion.7
  10.0 0.7 reduce.3
  10.9 0.6 reduce-window.16
  11.4 0.2 slice_reduce_fusion.1
  11.7 0.2 reduce-window.19
  11.9 24.6 %all_gather.9 = bf16[768,384]{1,0:T(8,128)(2,1)S(1)} all-gather(bf16[48,384]{1,0:T(8,128)(2,1)} %param.19), channel_id=1, replica_groups=mesh['req'=16,'head'=8] {'req'}, dimensions={0}, use_global_device_ids=true | all-gather | bytes 626688 | tf_op jit(solution)/shard_map/all_gather | solution.py:46
  36.5 23.5 %all_gather.10 = bf16[768,384]{1,0:T(8,128)(2,1)S(1)} all-gather(bf16[48,384]{1,0:T(8,128)(2,1)} %param.20), channel_id=1, replica_groups=mesh['req'=16,'head'=8] {'req'}, dimensions={0}, use_global_device_ids=true | all-gather | bytes 626688 | tf_op jit(solution)/shard_map/all_gather | solution.py:47
  60.0 21.9 %all_gather.11 = bf16[768,384]{1,0:T(8,128)(2,1)S(1)} all-gather(bf16[48,384]{1,0:T(8,128)(2,1)} %param.21), channel_id=1, replica_groups=mesh['req'=16,'head'=8] {'req'}, dimensions={0}, use_global_device_ids=true | all-gather | bytes 626688 | tf_op jit(solution)/shard_map/all_gather | solution.py:48
  82.1 0.4 convolution_convert_fusion.2
  82.5 0.2 copy-done.6
  82.7 0.7 slice_convert_fusion.2
  83.5 0.9 reshape.228
  84.6 1.0 reshape.234
  85.6 0.1 multiply_reduce_fusion.1
  85.7 1.1 copy.80
  86.8 1.0 reshape.232
  87.9 0.6 multiply_bitcast_fusion.1
  88.5 1.1 copy.73
  89.7 3.9 fusion.81
  93.5 2.6 copy.77
  96.2 1.8 convolution_multiply_fusion
  98.0 0.5 fusion.87
  98.5 0.2 divide_convert_fusion.2
  98.7 0.9 copy-done.3
  99.7 2.6 copy.70
  102.3 1.8 convolution_multiply_fusion.1
  104.1 0.5 fusion.88
  104.5 0.2 divide_convert_fusion.3
  104.7 0.9 copy-done.4
  105.7 0.5 copy-done.5
  106.2 1.9 fusion.82
  108.2 2.6 copy.81
  110.8 2.3 fusion.31
  113.3 2.7 copy.74
  115.9 2.3 fusion.32
  118.5 1.5 convolution_convert_fusion.3
  120.0 0.2 all-reduce.4.cloned.1.call-start
  120.9 0.6 iota_compare_fusion.5
  121.5 1.1 copy.86
  122.6 1.1 copy.85
  123.6 1.7 copy.84
  125.4 3.8 fusion.12
  129.2 4.9 %fusion.84 = f32[4,256]{1,0:T(4,128)S(1)} fusion(pred[256,2304]{0,1:T(8,128)(4,1)} %fusion.12, bf16[256,4,96]{0,2,1:T(8,128)(2,1)S(1)} %bitcast.97, bf16[256,4,96]{0,2,1:T(8,128)(2,1)S(1)} %bitcast.99, bf16[2048,4,96]{0,2,1:T(8,128)(2,1)} %bitcast.90), kind=kOutput, calls=%fused_computation.125 | convolution fusion | flops 465963264 | bytes 2560000 | tf_op jit(solution)/shard_map/sub | solution.py:19
  134.0 7.6 %fusion.28 = bf16[4,96,256]{2,1,0:T(8,128)(2,1)} fusion(f32[4,256]{1,0:T(4,128)S(1)} %fusion.84, bf16[256,4,96]{0,2,1:T(8,128)(2,1)} %bitcast.101, bf16[2048,4,96]{0,2,1:T(8,128)(2,1)} %bitcast.93, pred[256,2304]{0,1:T(8,128)(4,1)} %fusion.12, bf16[256,4,96]{0,2,1:T(8,128)(2,1)S(1)} %bitcast.98, bf16[256,4,96]{0,2,1:T(8,128)(2,1)S(1)} %bitcast.100, ...), kind=kOutput, calls=%fused_computation.45 | convolution fusion | flops 924945664 | bytes 4526080 | tf_op jit(solution)/shard_map/hqk,khd->qhd/dot_general | solution.py:123
  141.7 51.4 %reduce-scatter.7.cloned.1.call-done = bf16[48,384]{1,0:T(8,128)(2,1)} async-done(((bf16[768,384]{1,0:T(8,128)(2,1)}), bf16[48,384]{1,0:T(8,128)(2,1)}) %reduce-scatter.7.cloned.1.call-update) | async-done | bytes 36880
  193.0 0.9 copy.88
  193.9 3.1 fusion.44
  197.1 1.5 convert_element_type.133
  198.6 0.3 reduce-scatter.5.cloned.1.call-start
  198.9 0.9 reduce-window.14
  199.8 0.2 slice_reduce_fusion
  200.2 63.4 %all-reduce.4.cloned.1.call-done = bf16[304,3072]{1,0:T(8,128)(2,1)} async-done(((bf16[304,3072]{1,0:T(8,128)(2,1)}), bf16[304,3072]{1,0:T(8,128)(2,1)}) %all-reduce.4.cloned.1.call-update) | async-done | bytes 1867792 | tf_op jit(solution)/shard_map/psum | solution.py:146
  263.6 3.7 convolution_convert_fusion.1
  267.3 52.8 %all_to_all.9 = bf16[16,40,3072]{2,1,0:T(8,128)(2,1)S(1)} all-to-all(bf16[16,40,3072]{2,1,0:T(8,128)(2,1)S(1)} %bitcast.96), channel_id=1, replica_groups=mesh['req'=16,'head'=8] {'req'}, dimensions={0} | all-to-all | bytes 7864320 | tf_op jit(solution)/shard_map/all_to_all | solution.py:148
  320.1 0.8 multiply_reduce_fusion
  320.9 1.1 copy-done.1
  322.2 6.9 %multiply_convert_fusion = (bf16[640,3072]{1,0:T(8,128)(2,1)S(1)}, f32[16,40,3072]{2,1,0:T(8,128)}) fusion(f32[3072]{0:T(1024)S(1)} %copy-done.10, f32[640]{0:T(1024)S(1)} %rsqrt.12, bf16[16,40,3072]{2,1,0:T(8,128)(2,1)} %copy-done.1), kind=kLoop, calls=%fused_computation.7 | loop fusion | flops 7864320 | bytes 15743488 | tf_op jit(solution)/shard_map/convert_element_type | solution.py:151
  329.1 2.0 copy-done.2
  331.1 3.2 fusion.89
  334.4 9.7 %convolution_convert_fusion = bf16[640,3072]{1,0:T(8,128)(2,1)} fusion(bf16[512,3072]{1,0:T(8,128)(2,1)S(1)} %copy-done, bf16[640,3072]{1,0:T(8,128)(2,1)} %copy-done.2, bf16[3072,512]{1,0:T(8,128)(2,1)} %param.34, f32[640,512]{1,0:T(8,128)} %fusion.89), kind=kOutput, calls=%fused_computation.9 | convolution fusion | flops 4030464000 | bytes 15466496 | tf_op jit(solution)/shard_map/dot_general | solution.py:157
  344.1 37.5 %reduce-scatter.5.cloned.1.call-done = bf16[80,3072]{1,0:T(8,128)(2,1)} async-done(((bf16[640,3072]{1,0:T(8,128)(2,1)}), bf16[80,3072]{1,0:T(8,128)(2,1)}) %reduce-scatter.5.cloned.1.call-update) | async-done | bytes 491536 | tf_op jit(solution)/shard_map/reduce_scatter | solution.py:156
  381.6 2.2 add_convert_fusion
  (57 shorter events, 1.8 us)
Async XLA Ops:
  6.5 327.8 %copy-start = (bf16[512,3072]{1,0:T(8,128)(2,1)S(1)}, bf16[512,3072]{1,0:T(8,128)(2,1)}, u32[]{:S(2)}) copy-start(bf16[512,3072]{1,0:T(8,128)(2,1)} %param.35) | copy-start | bytes 9437188
  6.5 186.5 %reduce-scatter.7.cloned.1.call-start = ((), (), s32[]{:S(2)}) async-start(), calls=%async_computation.5 | async-start | bytes 626688
  82.1 0.6 copy-start.6
  96.2 1.8 copy-start.11
  96.2 1.8 copy-start.9
  98.7 0.9 copy-start.3
  104.0 2.2 copy-start.5
  104.7 0.9 copy-start.4
  115.9 2.5 copy-start.7
  115.9 4.9 %copy-start.12 = (s32[304,1]{0,1:T(1,128)S(1)}, s32[304,1]{0,1:T(1,128)}, u32[]{:S(2)}) copy-start(s32[304,1]{0,1:T(1,128)} %param.30) | copy-start | bytes 3652
  120.0 143.6 %all-reduce.4.cloned.1.call-start = ((), (), s32[]{:S(2)}) async-start(), calls=%async_computation.3 | async-start | bytes 3735552 | tf_op jit(solution)/shard_map/psum | solution.py:146
  193.9 3.1 copy-start.8
  198.6 182.9 %reduce-scatter.5.cloned.1.call-start = ((), (), s32[]{:S(2)}) async-start(), calls=%async_computation.4 | async-start | bytes 4423680 | tf_op jit(solution)/shard_map/reduce_scatter | solution.py:156
  320.1 2.0 copy-start.1
  320.1 2.1 copy-start.10
  322.2 8.9 %copy-start.13 = (bf16[3072,512]{1,0:T(8,128)(2,1)S(1)}, bf16[3072,512]{1,0:T(8,128)(2,1)}, u32[]{:S(2)}) copy-start(bf16[3072,512]{1,0:T(8,128)(2,1)} %param.33) | copy-start | bytes 9437188
  329.1 2.0 copy-start.2
Sparse Core Ops, SparseCore 0:
  120.1 72.9 reduce-scatter.6
  198.8 64.7 all-reduce.3
  344.2 37.3 reduce-scatter.4
where the time goes:
time: 392 us; the launch traced here: 390 us
  waiting for transfers between devices  152 us (39%)
  blocking collectives  123 us (31%)
  matrix products  42.3 us (11%)
  local copies, waits for them, and re-layouts  34.5 us (9%)
  other arithmetic  23.7 us (6%)
  between operations  14.1 us (4%)
    psum x1, waiting for transfers between devices, on_device(): residual = lax.psum(contribution.astype(jnp.bfloat16), 'head')  63.4 us
    all_to_all x1, blocking collectives, on_device(): lax.all_to_all(outgoing, 'req', split_axis=0, concat_axis=0, tiled=True)  52.8 us
    unnamed x4, waiting for transfers between devices  51.4 us
    reduce_scatter x1, waiting for transfers between devices, on_device(): lax.psum_scatter(jnp.dot(hidden, down_weight, preferred_element_type=jnp....  37.5 us
    all_gather x1, blocking collectives, on_device(): lax.all_gather(dec_query, 'req', axis=0, tiled=True)  24.6 us
    all_gather x1, blocking collectives, on_device(): lax.all_gather(dec_key, 'req', axis=0, tiled=True)  23.5 us
    all_gather x1, blocking collectives, on_device(): lax.all_gather(dec_value, 'req', axis=0, tiled=True)  21.9 us
    dot_general x1, matrix products, on_device(): jnp.dot(hidden, down_weight, preferred_element_type=jnp.float32)  9.69 us
  transfers between devices with their start and end apart: 3, of which 3 were waited for; matrix products, arithmetic and copies ran while one was open for 6% of the time, Pallas kernels for 0%

commit v1 on v0

--- a/solution.py
+++ b/solution.py
@@ -143,7 +143,12 @@
     placing = (
         target[None, :] == jnp.arange(req_count * slot_rows, dtype=jnp.int32)[:, None]
     ).astype(jnp.bfloat16)
-    residual = lax.psum(contribution.astype(jnp.bfloat16), "head")
+
+    def meet_halves(raw, net_axis):
+        seen_now = lax.all_gather(raw, net_axis).sum(axis=0)
+        return seen_now
+
+    residual = meet_halves(contribution.astype(jnp.bfloat16), "head")
     outgoing = jnp.dot(placing, residual, preferred_element_type=jnp.float32).astype(jnp.bfloat16)
     arrived = lax.all_to_all(outgoing, "req", split_axis=0, concat_axis=0, tiled=True)
     arrived_wide = arrived.astype(jnp.float32)

time: 392 us -> 413 us (1.054)
  other arithmetic: 23.7 us -> 33.8 us
  waiting for transfers between devices: 152 us -> 161 us
    all_gather x0 -> x1, waiting for transfers between devices: none -> 75 us  [meet_halves(): seen_now = lax.all_gather(raw, net_axis).sum(axis=0)]
    psum x1 -> x0, waiting for transfers between devices: 63.4 us -> none  [on_device(): residual = lax.psum(contribution.astype(jnp.bfloat16), 'head')]
    reduce_sum x0 -> x1, other arithmetic: none -> 9.89 us  [meet_halves(): seen_now = lax.all_gather(raw, net_axis).sum(axis=0)]
  transfers between devices with their start and end apart: 3 -> 3, of which waited for: 3 -> 3; matrix products, arithmetic and copies ran while one was open for 6% -> 5% of each run, Pallas kernels for 0% -> 0%
where the time goes in v1:
time: 413 us; the launch traced here: 412 us
  waiting for transfers between devices  161 us (39%)
  blocking collectives  125 us (30%)
  matrix products  42.3 us (10%)
  local copies, waits for them, and re-layouts  34.9 us (8%)
  other arithmetic  33.8 us (8%)
  between operations  14.1 us (3%)
    all_gather x1, waiting for transfers between devices, meet_halves(): seen_now = lax.all_gather(raw, net_axis).sum(axis=0)  75 us
    all_to_all x1, blocking collectives, on_device(): lax.all_to_all(outgoing, 'req', split_axis=0, concat_axis=0, tiled=True)  55.1 us
    unnamed x4, waiting for transfers between devices  51.3 us
    reduce_scatter x1, waiting for transfers between devices, on_device(): lax.psum_scatter(jnp.dot(hidden, down_weight, preferred_element_type=jnp....  34.5 us
    all_gather x1, blocking collectives, on_device(): lax.all_gather(dec_query, 'req', axis=0, tiled=True)  24.6 us
    all_gather x1, blocking collectives, on_device(): lax.all_gather(dec_key, 'req', axis=0, tiled=True)  23.5 us
    all_gather x1, blocking collectives, on_device(): lax.all_gather(dec_value, 'req', axis=0, tiled=True)  21.9 us
    unnamed x32, local copies, waits for them, and re-layouts  9.93 us
  transfers between devices with their start and end apart: 3, of which 3 were waited for; matrix products, arithmetic and copies ran while one was open for 5% of the time, Pallas kernels for 0%

profile of v1, /device:TPU:0, one launch (start us, length us, event | category | flops | bytes accessed | tf_op | source)
XLA Modules:
  0.0 411.5 jit_solution(17405445527574301663)
XLA Ops:
  6.6 1.5 fusion.83
  8.1 0.7 iota_compare_fusion.8
  8.8 1.3 iota_compare_fusion.7
  10.0 0.7 reduce.4
  10.9 0.6 reduce-window.16
  11.4 0.2 slice_reduce_fusion.1
  11.7 0.2 reduce-window.19
  11.9 24.6 %all_gather.15 = bf16[768,384]{1,0:T(8,128)(2,1)S(1)} all-gather(bf16[48,384]{1,0:T(8,128)(2,1)} %param.19), channel_id=1, replica_groups=mesh['req'=16,'head'=8] {'req'}, dimensions={0}, use_global_device_ids=true | all-gather | bytes 626688 | tf_op jit(solution)/shard_map/all_gather | solution.py:46
  36.5 23.5 %all_gather.16 = bf16[768,384]{1,0:T(8,128)(2,1)S(1)} all-gather(bf16[48,384]{1,0:T(8,128)(2,1)} %param.20), channel_id=1, replica_groups=mesh['req'=16,'head'=8] {'req'}, dimensions={0}, use_global_device_ids=true | all-gather | bytes 626688 | tf_op jit(solution)/shard_map/all_gather | solution.py:47
  60.0 21.9 %all_gather.17 = bf16[768,384]{1,0:T(8,128)(2,1)S(1)} all-gather(bf16[48,384]{1,0:T(8,128)(2,1)} %param.21), channel_id=1, replica_groups=mesh['req'=16,'head'=8] {'req'}, dimensions={0}, use_global_device_ids=true | all-gather | bytes 626688 | tf_op jit(solution)/shard_map/all_gather | solution.py:48
  82.1 0.4 convolution_convert_fusion.2
  82.5 0.2 copy-done.6
  82.7 0.7 slice_convert_fusion.2
  83.5 0.9 reshape.228
  84.6 1.0 reshape.234
  85.7 1.1 copy.80
  86.8 1.0 reshape.232
  87.9 0.6 multiply_bitcast_fusion.1
  88.5 1.1 copy.73
  89.7 3.9 fusion.81
  93.5 2.6 copy.77
  96.2 1.8 convolution_multiply_fusion
  98.0 0.5 fusion.87
  98.5 0.2 divide_convert_fusion.2
  98.7 0.9 copy-done.3
  99.7 2.6 copy.70
  102.3 1.8 convolution_multiply_fusion.1
  104.1 0.5 fusion.88
  104.7 0.9 copy-done.4
  105.7 0.5 copy-done.5
  106.2 1.9 fusion.82
  108.2 2.6 copy.81
  110.8 2.3 fusion.31
  113.3 2.7 copy.74
  115.9 2.3 fusion.32
  118.4 1.5 convolution_convert_fusion.3
  120.0 0.2 all-gather.3.cloned.1.call-start
  120.8 0.6 iota_compare_fusion.5
  121.4 1.1 copy.86
  122.5 1.1 copy.85
  123.6 1.7 copy.84
  125.3 3.9 fusion.12
  129.3 4.9 %fusion.84 = f32[4,256]{1,0:T(4,128)S(1)} fusion(pred[256,2304]{0,1:T(8,128)(4,1)} %fusion.12, bf16[256,4,96]{0,2,1:T(8,128)(2,1)S(1)} %bitcast.99, bf16[256,4,96]{0,2,1:T(8,128)(2,1)S(1)} %bitcast.101, bf16[2048,4,96]{0,2,1:T(8,128)(2,1)} %bitcast.92), kind=kOutput, calls=%fused_computation.125 | convolution fusion | flops 465963264 | bytes 2560000 | tf_op jit(solution)/shard_map/sub | solution.py:19
  134.2 7.6 %fusion.28 = bf16[4,96,256]{2,1,0:T(8,128)(2,1)} fusion(f32[4,256]{1,0:T(4,128)S(1)} %fusion.84, bf16[256,4,96]{0,2,1:T(8,128)(2,1)} %bitcast.103, bf16[2048,4,96]{0,2,1:T(8,128)(2,1)} %bitcast.95, pred[256,2304]{0,1:T(8,128)(4,1)} %fusion.12, bf16[256,4,96]{0,2,1:T(8,128)(2,1)S(1)} %bitcast.100, bf16[256,4,96]{0,2,1:T(8,128)(2,1)S(1)} %bitcast.102, ...), kind=kOutput, calls=%fused_computation.45 | convolution fusion | flops 924945664 | bytes 4526080 | tf_op jit(solution)/shard_map/hqk,khd->qhd/dot_general | solution.py:123
  141.8 51.3 %reduce-scatter.7.cloned.1.call-done = bf16[48,384]{1,0:T(8,128)(2,1)} async-done(((bf16[768,384]{1,0:T(8,128)(2,1)}), bf16[48,384]{1,0:T(8,128)(2,1)}) %reduce-scatter.7.cloned.1.call-update) | async-done | bytes 36880
  193.0 0.9 copy.88
  193.9 3.1 fusion.44
  197.1 1.5 convert_element_type.135
  198.7 0.3 reduce-scatter.5.cloned.1.call-start
  198.9 0.4 copy-done.12
  199.4 0.9 reduce-window.14
  200.2 0.2 slice_reduce_fusion
  200.6 75.0 %all-gather.3.cloned.1.call-done = bf16[2432,3072]{1,0:T(8,128)(2,1)} async-done(((bf16[304,3072]{1,0:T(8,128)(2,1)}), bf16[2432,3072]{1,0:T(8,128)(2,1)}) %all-gather.3.cloned.1.call-update) | async-done | bytes 14942224 | tf_op jit(solution)/shard_map/all_gather | solution.py:148
  275.6 9.9 %reduce_sum.81 = bf16[304,3072]{1,0:T(8,128)(2,1)} reduce(bf16[8,304,3072]{2,1,0:T(8,128)(2,1)} %bitcast.89, bf16[]{:T(256)} %constant.57.clone.1), dimensions={0}, to_apply=%region_14.15 | reduce | flops 6537216 | bytes 16809986 | tf_op jit(solution)/shard_map/reduce_sum | solution.py:148
  285.5 3.7 convolution_convert_fusion.1
  289.2 55.1 %all_to_all.9 = bf16[16,40,3072]{2,1,0:T(8,128)(2,1)S(1)} all-to-all(bf16[16,40,3072]{2,1,0:T(8,128)(2,1)S(1)} %bitcast.98), channel_id=1, replica_groups=mesh['req'=16,'head'=8] {'req'}, dimensions={0} | all-to-all | bytes 7864320 | tf_op jit(solution)/shard_map/all_to_all | solution.py:153
  344.3 0.8 multiply_reduce_fusion
  345.2 1.1 copy-done.1
  346.4 6.9 %multiply_convert_fusion = (bf16[640,3072]{1,0:T(8,128)(2,1)S(1)}, f32[16,40,3072]{2,1,0:T(8,128)}) fusion(f32[3072]{0:T(1024)S(1)} %copy-done.10, f32[640]{0:T(1024)S(1)} %rsqrt.12, bf16[16,40,3072]{2,1,0:T(8,128)(2,1)} %copy-done.1), kind=kLoop, calls=%fused_computation.7 | loop fusion | flops 7864320 | bytes 15743488 | tf_op jit(solution)/shard_map/convert_element_type | solution.py:156
  353.4 2.0 copy-done.2
  355.3 3.2 fusion.89
  358.6 9.7 %convolution_convert_fusion = bf16[640,3072]{1,0:T(8,128)(2,1)} fusion(bf16[512,3072]{1,0:T(8,128)(2,1)S(1)} %copy-done, bf16[640,3072]{1,0:T(8,128)(2,1)} %copy-done.2, bf16[3072,512]{1,0:T(8,128)(2,1)} %param.34, f32[640,512]{1,0:T(8,128)} %fusion.89), kind=kOutput, calls=%fused_computation.9 | convolution fusion | flops 4030464000 | bytes 15466496 | tf_op jit(solution)/shard_map/dot_general | solution.py:162
  368.3 34.5 %reduce-scatter.5.cloned.1.call-done = bf16[80,3072]{1,0:T(8,128)(2,1)} async-done(((bf16[640,3072]{1,0:T(8,128)(2,1)}), bf16[80,3072]{1,0:T(8,128)(2,1)}) %reduce-scatter.5.cloned.1.call-update) | async-done | bytes 491536 | tf_op jit(solution)/shard_map/reduce_scatter | solution.py:161
  402.8 2.2 add_convert_fusion
  (58 shorter events, 2.1 us)
Async XLA Ops:
  6.5 352.0 %copy-start = (bf16[512,3072]{1,0:T(8,128)(2,1)S(1)}, bf16[512,3072]{1,0:T(8,128)(2,1)}, u32[]{:S(2)}) copy-start(bf16[512,3072]{1,0:T(8,128)(2,1)} %param.35) | copy-start | bytes 9437188
  6.5 186.5 %reduce-scatter.7.cloned.1.call-start = ((), (), s32[]{:S(2)}) async-start(), calls=%async_computation.5 | async-start | bytes 626688
  82.1 0.6 copy-start.6
  96.2 1.8 copy-start.11
  96.2 1.8 copy-start.9
  98.7 0.9 copy-start.3
  104.0 2.2 copy-start.5
  104.7 0.9 copy-start.4
  115.9 2.5 copy-start.7
  120.0 155.7 %all-gather.3.cloned.1.call-start = ((), (), s32[]{:S(2)}) async-start(), calls=%async_computation.4 | async-start | bytes 16809984 | tf_op jit(solution)/shard_map/all_gather | solution.py:148
  193.9 3.1 copy-start.8
  198.6 0.7 copy-start.12
  198.7 204.1 %reduce-scatter.5.cloned.1.call-start = ((), (), s32[]{:S(2)}) async-start(), calls=%async_computation.3 | async-start | bytes 4423680 | tf_op jit(solution)/shard_map/reduce_scatter | solution.py:161
  344.3 2.0 copy-start.1
  344.3 2.1 copy-start.10
  346.4 8.9 %copy-start.13 = (bf16[3072,512]{1,0:T(8,128)(2,1)S(1)}, bf16[3072,512]{1,0:T(8,128)(2,1)}, u32[]{:S(2)}) copy-start(bf16[3072,512]{1,0:T(8,128)(2,1)} %param.33) | copy-start | bytes 9437188
  353.4 2.0 copy-start.2
Sparse Core Ops, SparseCore 0:
  120.1 72.9 reduce-scatter.6
  198.8 76.8 all-gather.2
  368.4 34.2 reduce-scatter.4
